TPU v7x, 128 devices: a whole 4x4x4 slice. The times are simulated.
128 devices in a mesh: tile: 32 (over x_lo, y, z), src: 4 (over x_hi, core).
Axes of the slice: x: 4 (x_hi: 2, x_lo: 2; x = x_hi * 2 + x_lo), y: 4, z: 4, core: 2. Of those that a mesh axis runs over, the one named last changes fastest.
Arguments:
- tile_tokens: bfloat16 [32768, 2048], P(('tile', 'src')), may hold values from -6 to 6
- norm_gain: float32 [2048], replicated, may hold values from 0.25 to 2.5
- up_weight: bfloat16 [2048, 2816], P('tile'), may hold values from -0.125 to 0.125
- down_weight: bfloat16 [2816, 2048], P('tile'), may hold values from -0.109375 to 0.109375
- head_weight: bfloat16 [2048, 768], P(None, 'src'), may hold values from -0.125 to 0.125
- source_index: int32 [128, 2], replicated, may hold values from 0 to 96, as said below
- source_cutoff: int32 [128], replicated, may hold values from 8 to 16
- source_weight: float32 [128], replicated, may hold values from 0.3 to 3
Outputs:
- intensity: float32 [128, 4096], P(('tile', 'src'))
Inputs may be any that keep to these rules, and one draw needn't show every extreme that they name: `source_index`: in each aligned group of 4 source points the first has the least value of the group in both coordinates, the second lies exactly 32 beyond it in both, and every other lies within 32 of the first in both.
All inputs are finite; a program needn't handle non-finite values.
Results may differ from a plain program's by a relative error of at most 0.0007.
Values may be sent and summed in bfloat16 or wider, within the bound.
No kernel may reach another device: no remote copies, remote signals or barrier semaphores. Data moves between devices by JAX's collectives and lax.ppermute only.
A program may use at most 128 MiB of HBM per device.

v0:
```python
import math
import jax
import jax.numpy as jnp
from jax import lax
from jax.sharding import PartitionSpec as P

GRID = 16
SUB = 8
W = 32
REG = 64
PIX = 64
SRC_DEV = 4
PATCH = 256
ORD = 128


def dft_tables():
    frequency = jnp.arange(W, dtype=jnp.int32) - W // 2
    position = jnp.arange(PIX, dtype=jnp.int32)
    phase_turns = jnp.mod(frequency[:, None] * position[None, :], PIX).astype(jnp.float32)
    phase_angle = phase_turns * (2.0 * math.pi / PIX)
    cosine = jnp.cos(phase_angle)
    sine_table = jnp.sin(phase_angle)
    table_one = jnp.concatenate(
        [jnp.concatenate([cosine, sine_table], 1), jnp.concatenate([-sine_table, cosine], 1)], 0
    )
    table_two = jnp.concatenate(
        [
            jnp.concatenate([cosine.T, -sine_table.T], 1),
            jnp.concatenate([sine_table.T, cosine.T], 1),
        ],
        0,
    )
    return (table_one, table_two)


def pupil_mask(radius):
    frequency = jnp.arange(W, dtype=jnp.int32) - W // 2
    distance = frequency[:, None] * frequency[:, None] + frequency[None, :] * frequency[None, :]
    return (distance <= radius * radius).astype(jnp.bfloat16)


def source_power(window, table_one, table_two):
    tile_count = window.shape[0]
    split_parts = (
        window.reshape(tile_count, 6, 2, W, W)
        .transpose(0, 1, 3, 2, 4)
        .reshape(tile_count, 6, W, 2 * W)
    )
    half_field = jnp.einsum(
        "bcik,ky->bciy", split_parts.astype(jnp.float32), table_one, precision=lax.Precision.HIGHEST
    )
    half_field = (
        half_field.reshape(tile_count, 6, W, 2, PIX)
        .transpose(0, 1, 3, 2, 4)
        .reshape(tile_count, 6, 2 * W, PIX)
    )
    image_field = jnp.einsum(
        "pk,bcky->bcpy", table_two, half_field, precision=lax.Precision.HIGHEST
    )
    power_map = jnp.sum((image_field * image_field).reshape(tile_count, 12, PIX, PIX), axis=1)
    return power_map.reshape(tile_count, PIX * PIX)


def local(
    tile_tokens,
    norm_gain,
    up_weight,
    down_weight,
    head_weight,
    source_index,
    source_cutoff,
    source_weight,
):
    residual = tile_tokens.astype(jnp.float32)
    mean_square = jnp.mean(residual * residual, axis=1, keepdims=True)
    normed = (residual * lax.rsqrt(mean_square + 1e-05) * norm_gain).astype(jnp.bfloat16)
    token_count = tile_tokens.shape[0]
    columns = normed
    pre_act = jnp.dot(
        columns,
        lax.all_gather(up_weight, "tile", axis=0, tiled=True),
        preferred_element_type=jnp.float32,
    )
    hidden = jax.nn.gelu(pre_act).astype(jnp.bfloat16)
    columns = hidden
    branch_out = jnp.dot(
        columns,
        lax.all_gather(down_weight, "tile", axis=0, tiled=True),
        preferred_element_type=jnp.float32,
    )
    mixed = (residual + branch_out).astype(jnp.bfloat16)
    coeffs = jnp.dot(
        mixed,
        lax.all_gather(head_weight, "src", axis=1, tiled=True),
        preferred_element_type=jnp.float32,
    ).astype(jnp.bfloat16)
    tile_count = token_count // PATCH
    spectra = (
        coeffs.reshape(tile_count, GRID, GRID, 12, SUB, SUB)
        .transpose(0, 3, 1, 4, 2, 5)
        .reshape(tile_count, 12, ORD, ORD)
    )
    group_count = lax.axis_size("tile")
    my_group = lax.axis_index("tile")
    anchor_zero = jnp.zeros((), jnp.int32)
    local_weight = lax.dynamic_slice_in_dim(source_weight, my_group * SRC_DEV, SRC_DEV, 0)
    table_one, table_two = dft_tables()
    image_count = group_count * tile_count
    running = jnp.zeros((image_count, PIX * PIX), jnp.float32)
    corner = jnp.min(source_index.reshape(group_count, SRC_DEV, 2), axis=1)

    def cut_region(corner_at):
        return lax.dynamic_slice(
            spectra,
            (anchor_zero, anchor_zero, corner_at[0], corner_at[1]),
            (tile_count, 12, REG, REG),
        )

    cut_blocks = jax.vmap(cut_region)(corner).reshape(group_count, tile_count, 12, REG * REG)
    received = lax.all_to_all(cut_blocks, "tile", split_axis=0, concat_axis=1, tiled=True)
    region = received.reshape(image_count, 12, REG, REG)
    base_corner = lax.dynamic_index_in_dim(corner, my_group, 0, keepdims=False)
    local_index = (
        lax.dynamic_slice_in_dim(source_index, my_group * SRC_DEV, SRC_DEV, 0)
        - base_corner[None, :]
    )
    local_cutoff = lax.dynamic_slice_in_dim(source_cutoff, my_group * SRC_DEV, SRC_DEV, 0)

    def add_source(total, source_item):
        corner_at, radius, weight = source_item
        window = lax.dynamic_slice(
            region, (anchor_zero, anchor_zero, corner_at[0], corner_at[1]), (image_count, 12, W, W)
        ) * pupil_mask(radius)
        return (total + weight * source_power(window, table_one, table_two), None)

    image_sum, unused = lax.scan(add_source, running, (local_index, local_cutoff, local_weight))
    norm_scale = 1.0 / (6.0 * W * W * source_weight.shape[0])
    everything = lax.psum(image_sum, "tile")
    result = lax.dynamic_slice_in_dim(everything, my_group * tile_count, tile_count, 0)
    return result * norm_scale


def solution(mesh):
    return jax.shard_map(
        local,
        mesh=mesh,
        in_specs=(
            P(("tile", "src"), None),
            P(),
            P("tile", None),
            P("tile", None),
            P(None, "src"),
            P(),
            P(),
            P(),
        ),
        out_specs=P(("tile", "src"), None),
        check_vma=False,
    )
```

profile of v0, /device:TPU:0, one launch (start us, length us, event | category | flops | bytes accessed | tf_op | source)
XLA Modules:
  0.0 1103.8 jit_solution(1894265273519993116)
XLA Ops:
  11.3 174.9 %all-gather.4.cloned.1.call-done = bf16[2048,2816]{1,0:T(8,128)(2,1)} async-done(((bf16[64,2816]{1,0:T(8,128)(2,1)}), bf16[2048,2816]{1,0:T(8,128)(2,1)}) %all-gather.4.cloned.1.call-update) | async-done | bytes 11534352 | tf_op jit(solution)/shard_map/all_gather | solution.py:82
  186.2 174.7 %all-gather.6.cloned.1.call-done = bf16[2816,2048]{1,0:T(8,128)(2,1)} async-done(((bf16[88,2048]{1,0:T(8,128)(2,1)}), bf16[2816,2048]{1,0:T(8,128)(2,1)}) %all-gather.6.cloned.1.call-update) | async-done | bytes 11534352 | tf_op jit(solution)/shard_map/all_gather | solution.py:89
  360.9 14.3 %fusion.12 = bf16[256,2048]{1,0:T(8,128)(2,1)S(1)} fusion(bf16[2816,2048]{1,0:T(8,128)(2,1)} %all-gather.6.cloned.1.call-done, bf16[256,2048]{1,0:T(8,128)(2,1)} %param.10, bf16[2048,2816]{1,0:T(8,128)(2,1)} %all-gather.4.cloned.1.call-done, f32[2048]{0:T(1024)} %param.11, f32[256]{0:T(256)S(1)} %add_rsqrt_fusion), kind=kOutput, calls=%fused_computation.25 | convolution fusion | flops 5915738112 | bytes 25175040 | tf_op jit(solution)/shard_map/dot_general | solution.py:87
  375.2 18.3 %all-gather.8.cloned.1.call-done = bf16[2048,768]{0,1:T(8,128)(2,1)} async-done(((bf16[2048,192]{0,1:T(8,128)(2,1)}), bf16[2048,768]{0,1:T(8,128)(2,1)}) %all-gather.8.cloned.1.call-update) | async-done | bytes 3145744 | tf_op jit(solution)/shard_map/all_gather | solution.py:95
  393.5 2.9 convolution_convert_fusion
  396.6 2.1 reshape.116
  398.8 5.3 copy.23
  404.1 8.2 reshape.117
  412.3 87.3 %while.14 = (s32[]{:T(128)}, bf16[1,12,128,128]{3,2,1,0:T(8,128)(2,1)S(1)}, s32[32,4]{0,1:T(4,128)S(1)}, bf16[32,1,12,64,64]{4,3,2,1,0:T(8,128)(2,1)}, s32[]{:T(128)}) while((s32[]{:T(128)}, bf16[1,12,128,128]{3,2,1,0:T(8,128)(2,1)S(1)}, s32[32,4]{0,1:T(4,128)S(1)}, bf16[32,1,12,64,64]{4,3,2,1,0:T(8,128)(2,1)}, s32[]{:T(128)}) %tuple.54), condition=%wide.while_cond, body=%wide.while_body.sunk | while | flops 2 | bytes 296561 | solution.py:114
  418.4 2.1 bitcast_dynamic-update-slice_fusion.2
  437.5 2.1 bitcast_dynamic-update-slice_fusion.2
  453.9 2.1 bitcast_dynamic-update-slice_fusion.2
  475.7 2.1 bitcast_dynamic-update-slice_fusion.2
  494.8 2.1 bitcast_dynamic-update-slice_fusion.2
  499.6 9.7 reshape.154
  509.3 7.5 all-to-all-start
  518.0 53.1 %all-to-all-done = bf16[32,1,12,4096]{3,2,1,0:T(8,128)(2,1)} async-done(((bf16[32,1,12,4096]{3,2,1,0:T(8,128)(2,1)}), bf16[32,1,12,4096]{3,2,1,0:T(8,128)(2,1)}, u32[]{:S(2)}, u32[]{:S(2)}) %all-to-all-start) | async-done | bytes 3145760 | tf_op jit(solution)/shard_map/all_to_all | solution.py:121
  571.0 9.9 reshape.155
  581.0 206.1 %while.15 = (s32[]{:T(128)}, f32[32,4096]{1,0:T(8,128)}, f32[4]{0:T(128)S(1)}, s32[4,2]{0,1:T(2,128)S(1)}, bf16[32,12,64,64]{3,2,1,0:T(8,128)(2,1)}, /*index=5*/...) while((s32[]{:T(128)}, f32[32,4096]{1,0:T(8,128)}, ...), condition=%wide.region_4.5_spmd.clone, body=%wide.region_2.4_spmd.clone.sunk | while | flops 1816923136 | bytes 45421140 | solution.py:137
  587.2 4.7 dynamic-slice_multiply_fusion.3
  591.9 3.3 copy.38
  595.3 2.6 reshape.159
  597.9 4.1 fusion.74
  601.9 12.1 %multiply_bitcast_fusion.2 = f32[32,6,128,64]{2,3,1,0:T(8,128)} fusion(f32[32,6,64,64]{3,2,1,0:T(8,128)S(1)} %bitcast.81, f32[128,64]{0,1:T(8,128)S(1)} %get-tuple-element.322), kind=kOutput, calls=%fused_computation.2.clone.1 | convolution fusion | flops 1209532416 | bytes 9469952 | tf_op jit(solution)/shard_map/while/body/eval_jaxpr/pk,bcky->bcpy/dot_general | solution.py:58
  614.1 9.6 copy.39
  623.7 6.3 reduce_sum.25
  638.8 4.5 dynamic-slice_multiply_fusion.3
  643.3 3.3 copy.38
  646.6 2.6 reshape.159
  649.2 4.1 fusion.74
  653.3 12.1 %multiply_bitcast_fusion.2 = f32[32,6,128,64]{2,3,1,0:T(8,128)} fusion(f32[32,6,64,64]{3,2,1,0:T(8,128)S(1)} %bitcast.81, f32[128,64]{0,1:T(8,128)S(1)} %get-tuple-element.322), kind=kOutput, calls=%fused_computation.2.clone.1 | convolution fusion | flops 1209532416 | bytes 9469952 | tf_op jit(solution)/shard_map/while/body/eval_jaxpr/pk,bcky->bcpy/dot_general | solution.py:58
  665.5 9.6 copy.39
  675.0 6.3 reduce_sum.25
  690.1 4.7 dynamic-slice_multiply_fusion.3
  694.9 3.3 copy.38
  698.2 2.6 reshape.159
  700.8 4.1 fusion.74
  704.9 12.1 %multiply_bitcast_fusion.2 = f32[32,6,128,64]{2,3,1,0:T(8,128)} fusion(f32[32,6,64,64]{3,2,1,0:T(8,128)S(1)} %bitcast.81, f32[128,64]{0,1:T(8,128)S(1)} %get-tuple-element.322), kind=kOutput, calls=%fused_computation.2.clone.1 | convolution fusion | flops 1209532416 | bytes 9469952 | tf_op jit(solution)/shard_map/while/body/eval_jaxpr/pk,bcky->bcpy/dot_general | solution.py:58
  717.1 9.6 copy.39
  726.6 6.3 reduce_sum.25
  741.7 4.7 dynamic-slice_multiply_fusion.3
  746.5 3.3 copy.38
  749.8 2.6 reshape.159
  752.4 4.1 fusion.74
  756.5 12.1 %multiply_bitcast_fusion.2 = f32[32,6,128,64]{2,3,1,0:T(8,128)} fusion(f32[32,6,64,64]{3,2,1,0:T(8,128)S(1)} %bitcast.81, f32[128,64]{0,1:T(8,128)S(1)} %get-tuple-element.322), kind=kOutput, calls=%fused_computation.2.clone.1 | convolution fusion | flops 1209532416 | bytes 9469952 | tf_op jit(solution)/shard_map/while/body/eval_jaxpr/pk,bcky->bcpy/dot_general | solution.py:58
  768.6 9.6 copy.39
  778.2 6.3 reduce_sum.25
  787.1 308.6 %all-reduce.2.cloned.1.call-done = f32[32,4096]{1,0:T(8,128)} async-done(((f32[32,4096]{1,0:T(8,128)}), f32[32,4096]{1,0:T(8,128)}) %all-reduce.2.cloned.1.call-update) | async-done | bytes 524304 | tf_op jit(solution)/shard_map/psum | solution.py:139
  (179 shorter events, 99.9 us)
Async XLA Ops:
  6.5 179.7 %all-gather.4.cloned.1.call-start = ((), (), s32[]{:S(2)}) async-start(), calls=%async_computation.1 | async-start | bytes 11894784 | tf_op jit(solution)/shard_map/all_gather | solution.py:82
  7.3 353.7 %all-gather.6.cloned.1.call-start = ((), (), s32[]{:S(2)}) async-start(), calls=%async_computation.2 | async-start | bytes 11894784 | tf_op jit(solution)/shard_map/all_gather | solution.py:89
  8.0 385.5 %all-gather.8.cloned.1.call-start = ((), (), s32[]{:S(2)}) async-start(), calls=%async_computation.3 | async-start | bytes 3932160 | tf_op jit(solution)/shard_map/all_gather | solution.py:95
  509.3 7.8 copy-start.3
  509.3 7.9 copy-start.4
  509.3 8.5 copy-start.2
  509.3 61.7 %all-to-all-start = ((bf16[32,1,12,4096]{3,2,1,0:T(8,128)(2,1)}), bf16[32,1,12,4096]{3,2,1,0:T(8,128)(2,1)}, u32[]{:S(2)}, u32[]{:S(2)}) async-start(bf16[32,1,12,4096]{3,2,1,0:T(8,128)(2,1)} %bitcast.83), calls=%async_computation | async-start | bytes 8388608 | tf_op jit(solution)/shard_map/all_to_all | solution.py:121
  516.9 578.9 %all-reduce.2.cloned.1.call-start = ((), (), s32[]{:S(2)}) async-start(), calls=%async_computation.4 | async-start | bytes 1048576 | tf_op jit(solution)/shard_map/psum | solution.py:139
  629.9 1.7 copy-start
  631.7 0.8 copy-start.1
  681.3 1.7 copy-start
  683.1 0.8 copy-start.1
  732.9 1.7 copy-start
  734.7 0.8 copy-start.1
  784.5 1.7 copy-start
  786.3 0.8 copy-start.1
Sparse Core Ops, SparseCore 0:
  9.0 177.1 all-gather.3
  187.8 173.0 all-gather.5
  362.6 30.8 all-gather.7
  787.3 308.4 all-reduce.1
where the time goes:
time: 1110 us; the launch traced here: 1100 us
  waiting for transfers between devices  732 us (66%)
  local copies, waits for them, and re-layouts  198 us (18%)
  matrix products  82.1 us (7%)
  other arithmetic  51.2 us (5%)
  loops' own time  20 us (2%)
  between operations  13.3 us (1%)
    psum x1, waiting for transfers between devices, local(): everything = lax.psum(image_sum, 'tile')  309 us
    all_gather x1, waiting for transfers between devices, local(): lax.all_gather(up_weight, 'tile', axis=0, tiled=True)  175 us
    all_gather x1, waiting for transfers between devices, local(): lax.all_gather(down_weight, 'tile', axis=0, tiled=True)  175 us
    gather x96, local copies, waits for them, and re-layouts  87.2 us
    all_to_all x1, waiting for transfers between devices, local(): lax.all_to_all(cut_blocks, 'tile', split_axis=0, concat_axis=1, tiled=True)  53.1 us
    dot_general x4, matrix products, source_power(): jnp.einsum('pk,bcky->bcpy', table_two, half_field, precision=lax.Precisio...  48.6 us
    mul x4, local copies, waits for them, and re-layouts, source_power(): image_field * image_field  38.2 us
    reduce_sum x4, other arithmetic, source_power(): jnp.sum((image_field * image_field).reshape(tile_count, 12, PIX, PIX), ax...  25 us
  transfers between devices with their start and end apart: 5, of which 5 were waited for; matrix products, arithmetic and copies ran while one was open for 2% of the time, Pallas kernels for 0%

commit v1 on v0

--- a/solution.py
+++ b/solution.py
@@ -136,7 +136,7 @@
 
     image_sum, unused = lax.scan(add_source, running, (local_index, local_cutoff, local_weight))
     norm_scale = 1.0 / (6.0 * W * W * source_weight.shape[0])
-    everything = lax.psum(image_sum, "tile")
+    everything = jnp.sum(lax.all_gather(image_sum, "tile"), axis=0)
     result = lax.dynamic_slice_in_dim(everything, my_group * tile_count, tile_count, 0)
     return result * norm_scale
 

time: 1110 us -> 999 us (0.900)
  waiting for transfers between devices: 732 us -> 618 us
    psum x1 -> x0, waiting for transfers between devices: 309 us -> none  [local(): everything = lax.psum(image_sum, 'tile')]
    all_gather x0 -> x1, waiting for transfers between devices: none -> 195 us  [local(): everything = jnp.sum(lax.all_gather(image_sum, 'tile'), axis=0)]
where the time goes in v1:
time: 999 us; the launch traced here: 996 us
  waiting for transfers between devices  618 us (62%)
  local copies, waits for them, and re-layouts  198 us (20%)
  matrix products  82.1 us (8%)
  other arithmetic  56.9 us (6%)
  loops' own time  20 us (2%)
  between operations  13.3 us (1%)
    all_gather x1, waiting for transfers between devices, local(): everything = jnp.sum(lax.all_gather(image_sum, 'tile'), axis=0)  195 us
    all_gather x1, waiting for transfers between devices, local(): lax.all_gather(up_weight, 'tile', axis=0, tiled=True)  175 us
    all_gather x1, waiting for transfers between devices, local(): lax.all_gather(down_weight, 'tile', axis=0, tiled=True)  175 us
    gather x96, local copies, waits for them, and re-layouts  87.2 us
    all_to_all x1, waiting for transfers between devices, local(): lax.all_to_all(cut_blocks, 'tile', split_axis=0, concat_axis=1, tiled=True)  53.1 us
    dot_general x4, matrix products, source_power(): jnp.einsum('pk,bcky->bcpy', table_two, half_field, precision=lax.Precisio...  48.6 us
    mul x4, local copies, waits for them, and re-layouts, source_power(): image_field * image_field  38.2 us
    reduce_sum x4, other arithmetic, source_power(): jnp.sum((image_field * image_field).reshape(tile_count, 12, PIX, PIX), ax...  25 us
  transfers between devices with their start and end apart: 5, of which 5 were waited for; matrix products, arithmetic and copies ran while one was open for 2% of the time, Pallas kernels for 0%

profile of v1, /device:TPU:0, one launch (start us, length us, event | category | flops | bytes accessed | tf_op | source)
XLA Modules:
  0.0 995.9 jit_solution(17701228391624291919)
XLA Ops:
  11.3 174.9 %all-gather.6.cloned.1.call-done = bf16[2048,2816]{1,0:T(8,128)(2,1)} async-done(((bf16[64,2816]{1,0:T(8,128)(2,1)}), bf16[2048,2816]{1,0:T(8,128)(2,1)}) %all-gather.6.cloned.1.call-update) | async-done | bytes 11534352 | tf_op jit(solution)/shard_map/all_gather | solution.py:82
  186.2 174.7 %all-gather.8.cloned.1.call-done = bf16[2816,2048]{1,0:T(8,128)(2,1)} async-done(((bf16[88,2048]{1,0:T(8,128)(2,1)}), bf16[2816,2048]{1,0:T(8,128)(2,1)}) %all-gather.8.cloned.1.call-update) | async-done | bytes 11534352 | tf_op jit(solution)/shard_map/all_gather | solution.py:89
  360.9 14.3 %fusion.12 = bf16[256,2048]{1,0:T(8,128)(2,1)S(1)} fusion(bf16[2816,2048]{1,0:T(8,128)(2,1)} %all-gather.8.cloned.1.call-done, bf16[256,2048]{1,0:T(8,128)(2,1)} %param.10, bf16[2048,2816]{1,0:T(8,128)(2,1)} %all-gather.6.cloned.1.call-done, f32[2048]{0:T(1024)} %param.11, f32[256]{0:T(256)S(1)} %add_rsqrt_fusion), kind=kOutput, calls=%fused_computation.25 | convolution fusion | flops 5915738112 | bytes 25175040 | tf_op jit(solution)/shard_map/dot_general | solution.py:87
  375.2 18.3 %all-gather.10.cloned.1.call-done = bf16[2048,768]{0,1:T(8,128)(2,1)} async-done(((bf16[2048,192]{0,1:T(8,128)(2,1)}), bf16[2048,768]{0,1:T(8,128)(2,1)}) %all-gather.10.cloned.1.call-update) | async-done | bytes 3145744 | tf_op jit(solution)/shard_map/all_gather | solution.py:95
  393.5 2.9 convolution_convert_fusion
  396.6 2.1 reshape.116
  398.8 5.3 copy.23
  404.1 8.2 reshape.117
  412.3 87.3 %while.14 = (s32[]{:T(128)}, bf16[1,12,128,128]{3,2,1,0:T(8,128)(2,1)S(1)}, s32[32,4]{0,1:T(4,128)S(1)}, bf16[32,1,12,64,64]{4,3,2,1,0:T(8,128)(2,1)}, s32[]{:T(128)}) while((s32[]{:T(128)}, bf16[1,12,128,128]{3,2,1,0:T(8,128)(2,1)S(1)}, s32[32,4]{0,1:T(4,128)S(1)}, bf16[32,1,12,64,64]{4,3,2,1,0:T(8,128)(2,1)}, s32[]{:T(128)}) %tuple.54), condition=%wide.while_cond, body=%wide.while_body.sunk | while | flops 2 | bytes 296561 | solution.py:114
  418.4 2.1 bitcast_dynamic-update-slice_fusion.2
  437.5 2.1 bitcast_dynamic-update-slice_fusion.2
  453.9 2.1 bitcast_dynamic-update-slice_fusion.2
  475.7 2.1 bitcast_dynamic-update-slice_fusion.2
  499.6 9.7 reshape.155
  509.3 7.5 all-to-all-start
  518.0 53.1 %all-to-all-done = bf16[32,1,12,4096]{3,2,1,0:T(8,128)(2,1)} async-done(((bf16[32,1,12,4096]{3,2,1,0:T(8,128)(2,1)}), bf16[32,1,12,4096]{3,2,1,0:T(8,128)(2,1)}, u32[]{:S(2)}, u32[]{:S(2)}) %all-to-all-start) | async-done | bytes 3145760 | tf_op jit(solution)/shard_map/all_to_all | solution.py:121
  571.0 9.9 reshape.156
  581.0 206.1 %while.15 = (s32[]{:T(128)}, f32[32,4096]{1,0:T(8,128)}, f32[4]{0:T(128)S(1)}, s32[4,2]{0,1:T(2,128)S(1)}, bf16[32,12,64,64]{3,2,1,0:T(8,128)(2,1)}, /*index=5*/...) while((s32[]{:T(128)}, f32[32,4096]{1,0:T(8,128)}, ...), condition=%wide.region_4.5_spmd.clone, body=%wide.region_2.4_spmd.clone.sunk | while | flops 1816923136 | bytes 45421140 | solution.py:137
  587.2 4.7 dynamic-slice_multiply_fusion.3
  591.9 3.3 copy.38
  595.3 2.6 reshape.160
  597.9 4.1 fusion.74
  601.9 12.1 %multiply_bitcast_fusion.2 = f32[32,6,128,64]{2,3,1,0:T(8,128)} fusion(f32[32,6,64,64]{3,2,1,0:T(8,128)S(1)} %bitcast.82, f32[128,64]{0,1:T(8,128)S(1)} %get-tuple-element.322), kind=kOutput, calls=%fused_computation.2.clone.1 | convolution fusion | flops 1209532416 | bytes 9469952 | tf_op jit(solution)/shard_map/while/body/eval_jaxpr/pk,bcky->bcpy/dot_general | solution.py:58
  614.1 9.6 copy.39
  623.7 6.3 reduce_sum.35
  638.8 4.5 dynamic-slice_multiply_fusion.3
  643.3 3.3 copy.38
  646.6 2.6 reshape.160
  649.2 4.1 fusion.74
  653.3 12.1 %multiply_bitcast_fusion.2 = f32[32,6,128,64]{2,3,1,0:T(8,128)} fusion(f32[32,6,64,64]{3,2,1,0:T(8,128)S(1)} %bitcast.82, f32[128,64]{0,1:T(8,128)S(1)} %get-tuple-element.322), kind=kOutput, calls=%fused_computation.2.clone.1 | convolution fusion | flops 1209532416 | bytes 9469952 | tf_op jit(solution)/shard_map/while/body/eval_jaxpr/pk,bcky->bcpy/dot_general | solution.py:58
  665.5 9.6 copy.39
  675.0 6.3 reduce_sum.35
  690.1 4.7 dynamic-slice_multiply_fusion.3
  694.9 3.3 copy.38
  698.2 2.6 reshape.160
  700.8 4.1 fusion.74
  704.9 12.1 %multiply_bitcast_fusion.2 = f32[32,6,128,64]{2,3,1,0:T(8,128)} fusion(f32[32,6,64,64]{3,2,1,0:T(8,128)S(1)} %bitcast.82, f32[128,64]{0,1:T(8,128)S(1)} %get-tuple-element.322), kind=kOutput, calls=%fused_computation.2.clone.1 | convolution fusion | flops 1209532416 | bytes 9469952 | tf_op jit(solution)/shard_map/while/body/eval_jaxpr/pk,bcky->bcpy/dot_general | solution.py:58
  717.1 9.6 copy.39
  726.6 6.3 reduce_sum.35
  741.7 4.7 dynamic-slice_multiply_fusion.3
  746.5 3.3 copy.38
  749.8 2.6 reshape.160
  752.4 4.1 fusion.74
  756.5 12.1 %multiply_bitcast_fusion.2 = f32[32,6,128,64]{2,3,1,0:T(8,128)} fusion(f32[32,6,64,64]{3,2,1,0:T(8,128)S(1)} %bitcast.82, f32[128,64]{0,1:T(8,128)S(1)} %get-tuple-element.322), kind=kOutput, calls=%fused_computation.2.clone.1 | convolution fusion | flops 1209532416 | bytes 9469952 | tf_op jit(solution)/shard_map/while/body/eval_jaxpr/pk,bcky->bcpy/dot_general | solution.py:58
  768.6 9.6 copy.39
  778.2 6.3 reduce_sum.35
  787.1 195.0 %all-gather.12.cloned.1.call-done = f32[1024,4096]{1,0:T(8,128)} async-done(((f32[32,4096]{1,0:T(8,128)}), f32[1024,4096]{1,0:T(8,128)}) %all-gather.12.cloned.1.call-update) | async-done | bytes 16777232 | tf_op jit(solution)/shard_map/all_gather | solution.py:139
  982.1 6.6 reduce_sum.31
  (180 shorter events, 101.1 us)
Async XLA Ops:
  6.5 179.7 %all-gather.6.cloned.1.call-start = ((), (), s32[]{:S(2)}) async-start(), calls=%async_computation.1 | async-start | bytes 11894784 | tf_op jit(solution)/shard_map/all_gather | solution.py:82
  7.3 353.7 %all-gather.8.cloned.1.call-start = ((), (), s32[]{:S(2)}) async-start(), calls=%async_computation.2 | async-start | bytes 11894784 | tf_op jit(solution)/shard_map/all_gather | solution.py:89
  8.0 385.5 %all-gather.10.cloned.1.call-start = ((), (), s32[]{:S(2)}) async-start(), calls=%async_computation.3 | async-start | bytes 3932160 | tf_op jit(solution)/shard_map/all_gather | solution.py:95
  509.3 7.8 copy-start.3
  509.3 7.9 copy-start.4
  509.3 8.5 copy-start.2
  509.3 61.7 %all-to-all-start = ((bf16[32,1,12,4096]{3,2,1,0:T(8,128)(2,1)}), bf16[32,1,12,4096]{3,2,1,0:T(8,128)(2,1)}, u32[]{:S(2)}, u32[]{:S(2)}) async-start(bf16[32,1,12,4096]{3,2,1,0:T(8,128)(2,1)} %bitcast.85), calls=%async_computation | async-start | bytes 8388608 | tf_op jit(solution)/shard_map/all_to_all | solution.py:121
  516.9 465.2 %all-gather.12.cloned.1.call-start = ((), (), s32[]{:S(2)}) async-start(), calls=%async_computation.4 | async-start | bytes 17301504 | tf_op jit(solution)/shard_map/all_gather | solution.py:139
  629.9 1.7 copy-start
  631.7 0.8 copy-start.1
  681.3 1.7 copy-start
  683.1 0.8 copy-start.1
  732.9 1.7 copy-start
  734.7 0.8 copy-start.1
  784.5 1.7 copy-start
  786.3 0.8 copy-start.1
Sparse Core Ops, SparseCore 0:
  9.0 177.1 all-gather.5
  187.8 173.0 all-gather.7
  362.6 30.8 all-gather.9
  787.3 194.7 all-gather.11
